TPU v7x, 256 devices: a whole 4x4x8 slice. The times are simulated.
256 devices in a mesh: dp: 8 (over y, core), mp: 32 (over z, x).
Axes of the slice: x: 4, y: 4, z: 8, core: 2. Of those that a mesh axis runs over, the one named last changes fastest.
Arguments:
- table: bfloat16 [32, 2048, 128], P('mp'), may hold values from -6 to 6
- ids: int32 [65536, 32, 2], P('dp', 'mp'), may hold values from 0 to 2047
- counts: int32 [256, 8], P(('dp', 'mp')), may hold values from 1 to 96, 256 in all within a row
- labels: int32 [65536], P(('dp', 'mp')), may hold values from 0 to 4
- request_home: int32 [2048], replicated, may hold values from 0 to 2047, each once
- user_codes: bfloat16 [2048, 1024], P('dp'), may hold values from -6 to 6
- cross_down: bfloat16 [4096, 256], replicated, may hold values from -0.09375 to 0.09375
- cross_up: bfloat16 [256, 4096], replicated, may hold values from -0.375 to 0.375
- cross_bias: float32 [4096], replicated, may hold values from -4 to 4
- tower_weight: bfloat16 [4096, 1024], P('mp'), may hold values from -0.09375 to 0.09375
- tower_bias: float32 [1024], replicated, may hold values from -3 to 3
Outputs:
- scores: float32 [65536], P(('dp', 'mp'))
- pooled_grad: bfloat16 [65536, 32, 128], P('dp', 'mp')
Inputs may be any that keep to these rules, and one draw needn't show every extreme that they name: `counts`: each row sums to 256; its largest entry is exactly 96. `request_home`: a permutation of the request slots.
All inputs are finite; a program needn't handle non-finite values.
Results may differ from a plain program's by a relative error of at most 0.0097.
Values may be sent and summed in bfloat16 or wider, within the bound.
No kernel may reach another device: no remote copies, remote signals or barrier semaphores. Data moves between devices by JAX's collectives and lax.ppermute only.
A program may use at most 128 MiB of HBM per device.

v0:
```python
import jax
import jax.numpy as jnp
from jax import lax
from jax.sharding import PartitionSpec as P


def members(counts_row, rows):
    ends = jnp.cumsum(counts_row)
    starts = ends - counts_row
    place = jnp.arange(rows, dtype=jnp.int32)[:, None]
    return (place >= starts[None, :]) & (place < ends[None, :])


def dot_last(left, right):
    return lax.dot_general(
        left, right, (((1,), (1,)), ((), ())), preferred_element_type=jnp.float32
    )


def pair_grad(scores, member, labels):
    gain = jnp.exp2(labels.astype(jnp.float32))
    member_f = member.astype(jnp.float32)
    same = jnp.dot(member_f, member_f.T) > 0.5
    diff = gain[:, None] - gain[None, :]
    gap = scores[None, :] - scores[:, None]
    turn = jnp.where(diff > 0, jax.nn.sigmoid(gap), jax.nn.sigmoid(-gap))
    total = jnp.sum(jnp.where(same, diff * turn, 0.0), axis=1)
    seg_gain = jnp.sum(jnp.where(member, (gain - 1.0)[:, None], 0.0), axis=0)
    norm = jnp.sum(jnp.where(member, seg_gain[None, :], 0.0), axis=1)
    return -total / jnp.maximum(norm, 1.0)


def local(
    table,
    ids,
    counts,
    labels,
    request_home,
    user_codes,
    cross_down,
    cross_up,
    cross_bias,
    tower_weight,
    tower_bias,
):
    f32, bf16 = (jnp.float32, jnp.bfloat16)
    n_mp = lax.axis_size("mp")
    n_dp = lax.axis_size("dp")
    d_idx = lax.axis_index("dp")
    m_idx = lax.axis_index("mp")
    rows = labels.shape[0]
    seg_count = counts.shape[1]
    width = user_codes.shape[1]
    emb = table.shape[2]
    rank = cross_down.shape[1]
    scale = 1.0 / jnp.sqrt(jnp.float32(width))
    piece = tower_weight.shape[1] // n_dp
    w_piece = lax.dynamic_slice_in_dim(tower_weight, d_idx * piece, piece, axis=1)
    w_cols = lax.all_gather(w_piece, "mp", axis=0, tiled=True)
    w_all = lax.all_gather(w_cols, "dp", axis=1, tiled=True)
    w3 = w_all.reshape(n_mp, emb, width)
    held = user_codes.shape[0]
    home_local = lax.dynamic_slice_in_dim(request_home, d_idx * held, held)
    wanted = (
        (jnp.arange(n_dp, dtype=jnp.int32)[:, None] * n_mp + m_idx) * seg_count
        + jnp.arange(seg_count, dtype=jnp.int32)[None, :]
    ).reshape(-1)
    pick = (home_local[None, :] == wanted[:, None]).astype(bf16)
    mine = jnp.dot(pick, user_codes, preferred_element_type=f32).astype(bf16)
    user_seg = lax.psum_scatter(
        mine.reshape(n_dp, seg_count, width), "dp", scatter_dimension=0, tiled=False
    )
    slab = table[0]
    picked = jnp.take(slab, ids[:, 0, :], axis=0, mode="clip")
    pooled = jnp.sum(picked.astype(f32), axis=1).astype(bf16)
    x0f = lax.all_to_all(
        pooled.reshape(n_mp, rows, emb), "mp", split_axis=0, concat_axis=0, tiled=True
    )
    member = members(counts[0], rows)
    cd3 = cross_down.reshape(n_mp, emb, rank)
    cu3 = cross_up.reshape(rank, n_mp, emb)
    bias3 = cross_bias.reshape(n_mp, 1, emb)
    z = jnp.einsum("fcd,fdr->cr", x0f, cd3, preferred_element_type=f32).astype(bf16)
    cross = jnp.einsum("cr,rfd->fcd", z, cu3, preferred_element_type=f32) + bias3
    x1 = (x0f * cross + x0f).astype(bf16)
    act = jnp.einsum("fcd,fdh->ch", x1, w3, preferred_element_type=f32) + tower_bias
    sig = jax.nn.sigmoid(act)
    hidden = (act * sig).astype(bf16)
    pair = dot_last(hidden, user_seg)
    score = jnp.sum(jnp.where(member, pair, 0.0), axis=1) * scale
    dscore = pair_grad(score, member, labels)
    code = jnp.dot(member.astype(bf16), user_seg, preferred_element_type=f32)
    slope = sig * (1.0 + act * (1.0 - sig))
    dact = (dscore[:, None] * code * scale * slope).astype(bf16)
    dx1 = jnp.einsum("ch,fdh->fcd", dact, w3, preferred_element_type=f32)
    dcross = (dx1 * x0f).astype(bf16)
    dz = jnp.einsum("fcd,rfd->cr", dcross, cu3, preferred_element_type=f32).astype(bf16)
    dx0 = dx1 * (1.0 + cross) + jnp.einsum("cr,fdr->fcd", dz, cd3, preferred_element_type=f32)
    grads = dx0.astype(bf16)
    returned = lax.all_to_all(grads, "mp", split_axis=0, concat_axis=0, tiled=True)
    return (score, returned.reshape(n_mp * rows, 1, emb))


def solution(mesh):
    in_specs = (
        P("mp", None, None),
        P("dp", "mp", None),
        P(("dp", "mp"), None),
        P(("dp", "mp")),
        P(),
        P("dp", None),
        P(),
        P(),
        P(),
        P("mp", None),
        P(),
    )
    out_specs = (P(("dp", "mp")), P("dp", "mp", None))
    return jax.shard_map(local, mesh=mesh, in_specs=in_specs, out_specs=out_specs, check_vma=False)
```

profile of v0, /device:TPU:10, one launch (start us, length us, event | category | flops | bytes accessed | tf_op | source)
XLA Modules:
  0.0 346.3 jit_solution(14947742715400940034)
XLA Ops:
  7.2 0.0 copy-start
  7.2 0.0 all-gather.3.cloned.1.call-start
  7.2 1.5 constant_dynamic-slice_fusion
  8.7 0.0 all-gather.3.cloned.1.call-update
  8.8 0.0 all-gather.5.cloned.1.call-start
  8.8 80.5 %all-gather.3.cloned.1.call-done = bf16[4096,128]{1,0:T(8,128)(2,1)} async-done(((bf16[128,128]{1,0:T(8,128)(2,1)}), bf16[4096,128]{1,0:T(8,128)(2,1)}) %all-gather.3.cloned.1.call-update) | async-done | bytes 1048592 | tf_op jit(solution)/shard_map/all_gather | solution.py:59
  89.3 0.0 all-gather.5.cloned.1.call-update
  89.3 3.4 copy.18
  92.7 0.0 copy-start.1
  92.7 4.1 %reshape.87 = s32[16384]{0:T(1024)S(1)} reshape(s32[8192,1,2]{2,0,1:T(8,128)} %copy.18) | data formatting | bytes 131072 | tf_op jit(solution)/shard_map/jit(_take)/broadcast_in_dim | solution.py:74
  96.8 0.0 copy-done.1
  96.8 57.8 %gather_fusion = bf16[16384,128]{1,0:T(8,128)(2,1)} fusion(bf16[2048,128]{1,0:T(8,128)(2,1)S(1)} %bitcast.114, s32[16384]{0:T(1024)S(1)} %broadcast_clamp_fusion), kind=kCustom, calls=%fused_computation | custom fusion | bytes 8454144 | tf_op jit(solution)/shard_map/jit(_take)/gather | solution.py:74
  154.6 45.8 %reduce_sum.48 = bf16[8192,128]{1,0:T(8,128)(2,1)} reduce(bf16[8192,2,128]{2,1,0:T(2,128)(2,1)} %bitcast.115, bf16[]{:T(256)} %constant.18.clone.1), dimensions={1}, to_apply=%region_1.2 | reduce | flops 1048576 | bytes 6291458 | tf_op jit(solution)/shard_map/reduce_sum | solution.py:75
  200.4 0.0 copy-start.2
  200.5 0.0 copy-start.8
  200.5 0.0 copy-start.4
  200.5 7.7 %all-to-all-start = ((bf16[32,256,128]{2,1,0:T(8,128)(2,1)}), bf16[32,256,128]{2,1,0:T(8,128)(2,1)}, u32[]{:S(2)}, u32[]{:S(2)}) async-start(bf16[32,256,128]{2,1,0:T(8,128)(2,1)} %bitcast.116), calls=%async_computation | async-start | bytes 4194304 | tf_op jit(solution)/shard_map/all_to_all | solution.py:76
  208.1 0.2 reduce-scatter.2.cloned.1.call-start
  208.4 0.1 iota_add_fusion
  208.4 0.1 add.100
  208.5 0.8 dynamic_slice.7
  209.3 0.0 copy-done.2
  209.3 0.9 fusion.36
  210.2 0.0 reduce-scatter.2.cloned.1.call-update
  210.2 0.0 copy-done.8
  210.2 0.2 reduce-window.4
  210.4 0.0 copy-done.4
  210.4 0.2 select_reduce_fusion.1
  210.6 0.1 select_reduce_fusion
  210.7 42.6 %all-to-all-done = bf16[32,256,128]{2,1,0:T(8,128)(2,1)} async-done(((bf16[32,256,128]{2,1,0:T(8,128)(2,1)}), bf16[32,256,128]{2,1,0:T(8,128)(2,1)}, u32[]{:S(2)}, u32[]{:S(2)}) %all-to-all-start) | async-done | bytes 2097184 | tf_op jit(solution)/shard_map/all_to_all | solution.py:76
  253.3 0.0 copy-done
  253.3 0.0 copy-start.3
  253.3 0.0 copy-start.7
  253.3 6.6 %fusion.8 = f32[256,32,128]{2,0,1:T(8,128)} fusion(bf16[32,256,128]{2,1,0:T(8,128)(2,1)} %all-to-all-done, bf16[32,128,256]{2,1,0:T(8,128)(2,1)S(1)} %bitcast.112, bf16[256,4096]{1,0:T(8,128)(2,1)} %param.18), kind=kOutput, calls=%fused_computation.12 | convolution fusion | flops 1073807360 | bytes 10485760 | tf_op jit(solution)/shard_map/cr,rfd->fcd/dot_general | solution.py:84
  259.9 0.0 all-gather.5.cloned.1.call-done
  259.9 0.0 copy-done.3
  259.9 0.0 copy-done.7
  259.9 6.7 %fusion.18 = f32[256,1024]{1,0:T(8,128)S(1)} fusion(bf16[32,128,1024]{2,1,0:T(8,128)(2,1)} %bitcast.125, bf16[32,256,128]{2,1,0:T(8,128)(2,1)} %all-to-all-done, f32[256,32,128]{2,0,1:T(8,128)} %fusion.8, f32[32,128]{1,0:T(8,128)S(1)} %bitcast.118, f32[1024]{0:T(1024)S(1)} %copy-done.7), kind=kOutput, calls=%fused_computation.21 | convolution fusion | flops 2152988672 | bytes 15749120 | tf_op jit(solution)/shard_map/fcd,fdh->ch/dot_general | solution.py:86
  266.6 0.0 reduce-scatter.2.cloned.1.call-done
  266.6 1.1 fusion.47
  267.8 0.0 copy-start.6
  267.8 0.0 copy-start.5
  267.8 0.4 fusion.35
  268.2 0.3 copy-done.6
  268.5 7.1 %fusion.48 = f32[32,128,256]{1,2,0:T(8,128)} fusion(bf16[32,128,1024]{2,1,0:T(8,128)(2,1)} %bitcast.126, f32[256,1024]{1,0:T(8,128)S(1)} %fusion.18, f32[256]{0:T(256)S(1)} %maximum_divide_fusion, bf16[1,8,1024]{2,1,0:T(8,128)(2,1)S(1)} %copy-done.6, s32[8]{0:T(128)S(1)} %bitcast.124, s32[8]{0:T(128)S(1)} %fusion.65), kind=kOutput, calls=%fused_computation.39 | convolution fusion | flops 2154567680 | bytes 13648960 | tf_op jit(solution)/shard_map/ch,fdh->fcd/dot_general | solution.py:95
  275.6 0.0 copy-done.5
  275.6 9.6 %fusion.2 = bf16[32,256,128]{2,1,0:T(8,128)(2,1)} fusion(f32[32,128,256]{1,2,0:T(8,128)} %fusion.48, f32[256,32,128]{2,0,1:T(8,128)} %fusion.8, bf16[32,128,256]{2,1,0:T(8,128)(2,1)S(1)} %bitcast.113, f32[32,128]{1,0:T(8,128)S(1)} %bitcast.119, bf16[32,256,128]{2,1,0:T(8,128)(2,1)} %all-to-all-done, bf16[256,4096]{1,0:T(8,128)(2,1)} %param.18), kind=kOutput, calls=%fused_computation.6 | convolution fusion | flops 1082195968 | bytes 16793600 | tf_op jit(solution)/shard_map/cr,fdr->fcd/dot_general | solution.py:98
  285.2 53.3 %all_to_all.10 = bf16[32,256,128]{2,1,0:T(8,128)(2,1)S(1)} all-to-all(bf16[32,256,128]{2,1,0:T(8,128)(2,1)} %fusion.2), channel_id=1, replica_groups=mesh['dp'=8,'mp'=32] {'mp'}, dimensions={0} | all-to-all | bytes 4194304 | tf_op jit(solution)/shard_map/all_to_all | solution.py:100
  338.4 1.3 copy.43
  (6 shorter events, 0.0 us)
Async XLA Ops:
  7.2 246.1 %copy-start = (bf16[4096,256]{1,0:T(8,128)(2,1)S(1)}, bf16[4096,256]{1,0:T(8,128)(2,1)}, u32[]{:S(2)}) copy-start(bf16[4096,256]{1,0:T(8,128)(2,1)} %param.17) | copy-start | bytes 6291460
  7.2 82.1 %all-gather.3.cloned.1.call-start = ((), (), s32[]{:S(2)}) async-start(), calls=%async_computation.3 | async-start | bytes 1081344 | tf_op jit(solution)/shard_map/all_gather | solution.py:59
  8.8 251.1 %all-gather.5.cloned.1.call-start = ((), (), s32[]{:S(2)}) async-start(), calls=%async_computation.4 | async-start | bytes 9437184 | tf_op jit(solution)/shard_map/all_gather | solution.py:60
  92.7 4.1 %copy-start.1 = (bf16[1,2048,128]{2,1,0:T(8,128)(2,1)S(1)}, bf16[1,2048,128]{2,1,0:T(8,128)(2,1)}, u32[]{:S(2)}) copy-start(bf16[1,2048,128]{2,1,0:T(8,128)(2,1)} %param.11) | copy-start | bytes 1572868
  200.4 8.8 %copy-start.2 = (bf16[256,1024]{1,0:T(8,128)(2,1)S(1)}, bf16[256,1024]{1,0:T(8,128)(2,1)}, u32[]{:S(2)}) copy-start(bf16[256,1024]{1,0:T(8,128)(2,1)} %param.16) | copy-start | bytes 1572868
  200.5 9.8 %copy-start.8 = (s32[1,8]{1,0:T(1,128)S(1)}, s32[1,8]{1,0:T(1,128)}, u32[]{:S(2)}) copy-start(s32[1,8]{1,0:T(1,128)} %param.13) | copy-start | bytes 100
  200.5 10.0 %copy-start.4 = (s32[256]{0:T(256)S(1)}, s32[256]{0:T(256)}, u32[]{:S(2)}) copy-start(s32[256]{0:T(256)} %param.14) | copy-start | bytes 3076
  200.5 52.8 %all-to-all-start = ((bf16[32,256,128]{2,1,0:T(8,128)(2,1)}), bf16[32,256,128]{2,1,0:T(8,128)(2,1)}, u32[]{:S(2)}, u32[]{:S(2)}) async-start(bf16[32,256,128]{2,1,0:T(8,128)(2,1)} %bitcast.116), calls=%async_computation | async-start | bytes 4194304 | tf_op jit(solution)/shard_map/all_to_all | solution.py:76
  208.1 58.5 %reduce-scatter.2.cloned.1.call-start = ((), (), s32[]{:S(2)}) async-start(), calls=%async_computation.5 | async-start | bytes 147456 | tf_op jit(solution)/shard_map/reduce_scatter | solution.py:70
  253.3 6.6 %copy-start.3 = (f32[4096]{0:T(1024)S(1)}, f32[4096]{0:T(1024)}, u32[]{:S(2)}) copy-start(f32[4096]{0:T(1024)} %param.19) | copy-start | bytes 49156
  253.3 6.6 %copy-start.7 = (f32[1024]{0:T(1024)S(1)}, f32[1024]{0:T(1024)}, u32[]{:S(2)}) copy-start(f32[1024]{0:T(1024)} %param.21) | copy-start | bytes 12292
  267.8 0.7 copy-start.6
  267.8 7.8 %copy-start.5 = (f32[256]{0:T(256)}, f32[256]{0:T(256)S(1)}, u32[]{:S(2)}) copy-start(f32[256]{0:T(256)S(1)} %broadcast_multiply_fusion) | copy-start | bytes 3076
Sparse Core Ops, SparseCore 0:
  11.1 78.0 all-gather.2
  91.1 54.5 all-gather.4
  211.4 31.8 reduce-scatter.1
where the time goes:
time: 347 us; the launch traced here: 346 us
  waiting for transfers between devices  123 us (35%)
  local copies, waits for them, and re-layouts  69.3 us (20%)
  blocking collectives  53.3 us (15%)
  other arithmetic  46.4 us (13%)
  matrix products  32.4 us (9%)
  between operations  13.9 us (4%)
  starting transfers between devices  7.95 us (2%)
    all_gather x1, waiting for transfers between devices, local(): w_cols = lax.all_gather(w_piece, 'mp', axis=0, tiled=True)  80.5 us
    gather x1, local copies, waits for them, and re-layouts, local(): picked = jnp.take(slab, ids[:, 0, :], axis=0, mode='clip')  57.8 us
    all_to_all x1, blocking collectives, local(): lax.all_to_all(grads, 'mp', split_axis=0, concat_axis=0, tiled=True)  53.3 us
    reduce_sum x1, other arithmetic, local(): pooled = jnp.sum(picked.astype(f32), axis=1).astype(bf16)  45.8 us
    all_to_all x1, waiting for transfers between devices, local(): lax.all_to_all(pooled.reshape(n_mp, rows, emb), 'mp', split_axis=0, conca...  42.6 us
    dot_general x1, matrix products, local(): jnp.einsum('cr,fdr->fcd', dz, cd3, preferred_element_type=f32)  9.56 us
    all_to_all x1, starting transfers between devices, local(): lax.all_to_all(pooled.reshape(n_mp, rows, emb), 'mp', split_axis=0, conca...  7.65 us
    dot_general x1, matrix products, local(): dx1 = jnp.einsum('ch,fdh->fcd', dact, w3, preferred_element_type=f32)  7.13 us
  transfers between devices with their start and end apart: 4, of which 2 were waited for; matrix products, arithmetic and copies ran while one was open for 37% of the time, Pallas kernels for 0%

commit v1 on v0

--- a/solution.py
+++ b/solution.py
@@ -57,7 +57,9 @@
     piece = tower_weight.shape[1] // n_dp
     w_piece = lax.dynamic_slice_in_dim(tower_weight, d_idx * piece, piece, axis=1)
     w_cols = lax.all_gather(w_piece, "mp", axis=0, tiled=True)
-    w_all = lax.all_gather(w_cols, "dp", axis=1, tiled=True)
+    w_all = jnp.concatenate(
+        lax.all_to_all(jnp.stack([w_cols] * lax.axis_size("dp")), "dp", 0, 0), axis=1
+    )
     w3 = w_all.reshape(n_mp, emb, width)
     held = user_codes.shape[0]
     home_local = lax.dynamic_slice_in_dim(request_home, d_idx * held, held)

time: 347 us -> 434 us (1.25)
  waiting for transfers between devices: 123 us -> 165 us
  local copies, waits for them, and re-layouts: 69.3 us -> 97.7 us
  starting transfers between devices: 7.95 us -> 17.2 us
  blocking collectives: 53.3 us -> 57.7 us
    all_to_all x0 -> x1, waiting for transfers between devices: none -> 85 us  [local(): lax.all_to_all(jnp.stack([w_cols] * lax.axis_size('dp')), 'dp', 0, 0)]
    all_to_all x1, waiting for transfers between devices: 42.6 us -> 0.01 us  [local(): lax.all_to_all(pooled.reshape(n_mp, rows, emb), 'mp', split_axis=0, conca...]
    another operation x0 -> x2, local copies, waits for them, and re-layouts: none -> 18.8 us  [the longest x1 13.3 us: local(): w3 = w_all.reshape(n_mp, emb, width)]
    reshape x0 -> x1, local copies, waits for them, and re-layouts: none -> 10.3 us  [local(): jnp.concatenate(lax.all_to_all(jnp.stack([w_cols] * lax.axis_size('dp')),...]
    all_to_all x0 -> x1, starting transfers between devices: none -> 5.51 us  [local(): lax.all_to_all(jnp.stack([w_cols] * lax.axis_size('dp')), 'dp', 0, 0)]
    all_to_all x1, blocking collectives: 53.3 us -> 57.7 us  [local(): lax.all_to_all(grads, 'mp', split_axis=0, concat_axis=0, tiled=True)]
  transfers between devices with their start and end apart: 4 -> 4, of which waited for: 2 -> 2; matrix products, arithmetic and copies ran while one was open for 37% -> 9% of each run, Pallas kernels for 0% -> 0%
where the time goes in v1:
time: 434 us; the launch traced here: 432 us
  waiting for transfers between devices  165 us (38%)
  local copies, waits for them, and re-layouts  97.7 us (23%)
  blocking collectives  57.7 us (13%)
  other arithmetic  46.4 us (11%)
  matrix products  32.5 us (7%)
  starting transfers between devices  17.2 us (4%)
  between operations  15.6 us (4%)
    all_to_all x1, waiting for transfers between devices, local(): lax.all_to_all(jnp.stack([w_cols] * lax.axis_size('dp')), 'dp', 0, 0)  85 us
    all_gather x1, waiting for transfers between devices, local(): w_cols = lax.all_gather(w_piece, 'mp', axis=0, tiled=True)  79.9 us
    all_to_all x1, blocking collectives, local(): lax.all_to_all(grads, 'mp', split_axis=0, concat_axis=0, tiled=True)  57.7 us
    gather x1, local copies, waits for them, and re-layouts, local(): picked = jnp.take(slab, ids[:, 0, :], axis=0, mode='clip')  57.4 us
    reduce_sum x1, other arithmetic, local(): pooled = jnp.sum(picked.astype(f32), axis=1).astype(bf16)  45.8 us
    another operation x1, local copies, waits for them, and re-layouts, local(): w3 = w_all.reshape(n_mp, emb, width)  13.3 us
    all_to_all x1, starting transfers between devices, local(): lax.all_to_all(pooled.reshape(n_mp, rows, emb), 'mp', split_axis=0, conca...  11.7 us
    reshape x1, local copies, waits for them, and re-layouts, local(): jnp.concatenate(lax.all_to_all(jnp.stack([w_cols] * lax.axis_size('dp')),...  10.3 us
  transfers between devices with their start and end apart: 4, of which 2 were waited for; matrix products, arithmetic and copies ran while one was open for 9% of the time, Pallas kernels for 0%

profile of v1, /device:TPU:10, one launch (start us, length us, event | category | flops | bytes accessed | tf_op | source)
XLA Modules:
  0.0 432.0 jit_solution(4329525168744055136)
XLA Ops:
  8.0 0.0 copy-start
  8.0 0.0 copy-start.1
  8.0 3.5 copy.18
  11.5 4.0 reshape.89
  15.6 0.0 copy-done.1
  15.6 57.4 %gather_fusion = bf16[16384,128]{1,0:T(8,128)(2,1)} fusion(bf16[2048,128]{1,0:T(8,128)(2,1)S(1)} %bitcast.114, s32[16384]{0:T(1024)S(1)} %broadcast_clamp_fusion), kind=kCustom, calls=%fused_computation | custom fusion | bytes 8454144 | tf_op jit(solution)/shard_map/jit(_take)/gather | solution.py:76
  73.0 45.8 %reduce_sum.48 = bf16[8192,128]{1,0:T(8,128)(2,1)} reduce(bf16[8192,2,128]{2,1,0:T(2,128)(2,1)} %bitcast.115, bf16[]{:T(256)} %constant.18.clone.1), dimensions={1}, to_apply=%region_1.2 | reduce | flops 1048576 | bytes 6291458 | tf_op jit(solution)/shard_map/reduce_sum | solution.py:77
  118.8 11.7 %all-to-all-start = ((bf16[32,256,128]{2,1,0:T(8,128)(2,1)}), bf16[32,256,128]{2,1,0:T(8,128)(2,1)}, u32[]{:S(2)}, u32[]{:S(2)}) async-start(bf16[32,256,128]{2,1,0:T(8,128)(2,1)} %bitcast.116), calls=%async_computation | async-start | bytes 4194304 | tf_op jit(solution)/shard_map/all_to_all | solution.py:78
  130.5 0.0 all-gather.2.cloned.1.call-start
  130.5 1.4 constant_dynamic-slice_fusion
  131.9 0.0 all-gather.2.cloned.1.call-update
  131.9 79.9 %all-gather.2.cloned.1.call-done = bf16[4096,128]{1,0:T(8,128)(2,1)} async-done(((bf16[128,128]{1,0:T(8,128)(2,1)}), bf16[4096,128]{1,0:T(8,128)(2,1)}) %all-gather.2.cloned.1.call-update) | async-done | bytes 1048592 | tf_op jit(solution)/shard_map/all_gather | solution.py:59
  211.8 0.0 all-to-all-done
  211.8 5.5 %stack.2 = bf16[8,4096,128]{2,1,0:T(8,128)(2,1)} broadcast(bf16[4096,128]{1,0:T(8,128)(2,1)} %all-gather.2.cloned.1.call-done), dimensions={1,2} | broadcast | bytes 9437184 | tf_op jit(solution)/shard_map/stack | solution.py:61
  217.3 0.0 copy-start.2
  217.3 0.0 copy-start.8
  217.3 0.0 copy-start.4
  217.3 5.5 %all-to-all-start.1 = ((bf16[8,4096,128]{2,1,0:T(8,128)(2,1)}), bf16[8,4096,128]{2,1,0:T(8,128)(2,1)}, u32[]{:S(2)}, u32[]{:S(2)}) async-start(bf16[8,4096,128]{2,1,0:T(8,128)(2,1)} %stack.2), calls=%async_computation.1 | async-start | bytes 16777216 | tf_op jit(solution)/shard_map/all_to_all | solution.py:61
  222.8 0.0 reduce-scatter.2.cloned.1.call-start
  222.8 0.1 iota_add_fusion
  222.9 0.1 add.100
  223.0 0.8 dynamic_slice.7
  223.8 0.0 copy-done.2
  223.8 0.9 fusion.36
  224.7 0.0 reduce-scatter.2.cloned.1.call-update
  224.7 0.0 copy-done.8
  224.7 0.2 reduce-window.4
  224.9 0.0 copy-done.4
  224.9 0.2 select_reduce_fusion.1
  225.1 0.1 select_reduce_fusion
  225.2 0.0 copy-done
  225.2 6.5 %fusion.8 = f32[256,32,128]{2,0,1:T(8,128)} fusion(bf16[32,256,128]{2,1,0:T(8,128)(2,1)} %all-to-all-done, bf16[32,128,256]{2,1,0:T(8,128)(2,1)S(1)} %bitcast.112, bf16[256,4096]{1,0:T(8,128)(2,1)} %param.18), kind=kOutput, calls=%fused_computation.12 | convolution fusion | flops 1073807360 | bytes 10485760 | tf_op jit(solution)/shard_map/cr,rfd->fcd/dot_general | solution.py:86
  231.7 85.0 %all-to-all-done.1 = bf16[8,4096,128]{2,1,0:T(8,128)(2,1)} async-done(((bf16[8,4096,128]{2,1,0:T(8,128)(2,1)}), bf16[8,4096,128]{2,1,0:T(8,128)(2,1)}, u32[]{:S(2)}, u32[]{:S(2)}) %all-to-all-start.1) | async-done | bytes 8388640 | tf_op jit(solution)/shard_map/all_to_all | solution.py:61
  316.7 10.3 %copy.20 = bf16[4096,8,128]{2,1,0:T(8,128)(2,1)} copy(bf16[4096,8,128]{2,0,1:T(8,128)(2,1)} %bitcast.12) | data formatting | bytes 16777216 | tf_op jit(solution)/shard_map/reshape | solution.py:60
  327.0 0.0 copy-start.3
  327.0 0.0 copy-start.7
  327.0 13.3 %reshape_reshape.3 = bf16[32,128,1024]{2,1,0:T(8,128)(2,1)} reshape(bf16[4096,8,128]{2,1,0:T(8,128)(2,1)} %copy.20) | data formatting | bytes 16777216 | tf_op jit(solution)/shard_map/reshape;reshape | solution.py:63
  340.4 0.0 copy-done.3
  340.4 0.0 copy-done.7
  340.4 6.7 %fusion.18 = f32[256,1024]{1,0:T(8,128)S(1)} fusion(bf16[32,128,1024]{2,1,0:T(8,128)(2,1)} %reshape_reshape.3, bf16[32,256,128]{2,1,0:T(8,128)(2,1)} %all-to-all-done, f32[256,32,128]{2,0,1:T(8,128)} %fusion.8, f32[32,128]{1,0:T(8,128)S(1)} %bitcast.118, f32[1024]{0:T(1024)S(1)} %copy-done.7), kind=kOutput, calls=%fused_computation.21 | convolution fusion | flops 2152988672 | bytes 15749120 | tf_op jit(solution)/shard_map/fcd,fdh->ch/dot_general | solution.py:88
  347.1 0.0 reduce-scatter.2.cloned.1.call-done
  347.1 0.0 copy-start.6
  347.1 1.2 fusion.47
  348.3 0.0 copy-start.5
  348.3 0.4 fusion.35
  348.7 0.0 copy-done.6
  348.7 7.1 %fusion.48 = f32[32,128,256]{1,2,0:T(8,128)} fusion(bf16[32,128,1024]{2,1,0:T(8,128)(2,1)} %reshape_reshape.3, f32[256,1024]{1,0:T(8,128)S(1)} %fusion.18, f32[256]{0:T(256)S(1)} %maximum_divide_fusion, bf16[1,8,1024]{2,1,0:T(8,128)(2,1)S(1)} %copy-done.6, s32[8]{0:T(128)S(1)} %bitcast.124, s32[8]{0:T(128)S(1)} %fusion.65), kind=kOutput, calls=%fused_computation.39 | convolution fusion | flops 2154567680 | bytes 13648960 | tf_op jit(solution)/shard_map/ch,fdh->fcd/dot_general | solution.py:97
  355.8 0.0 copy-done.5
  355.8 9.7 %fusion.2 = bf16[32,256,128]{2,1,0:T(8,128)(2,1)} fusion(f32[32,128,256]{1,2,0:T(8,128)} %fusion.48, f32[256,32,128]{2,0,1:T(8,128)} %fusion.8, bf16[32,128,256]{2,1,0:T(8,128)(2,1)S(1)} %bitcast.113, f32[32,128]{1,0:T(8,128)S(1)} %bitcast.119, bf16[32,256,128]{2,1,0:T(8,128)(2,1)} %all-to-all-done, bf16[256,4096]{1,0:T(8,128)(2,1)} %param.18), kind=kOutput, calls=%fused_computation.6 | convolution fusion | flops 1082195968 | bytes 16793600 | tf_op jit(solution)/shard_map/cr,fdr->fcd/dot_general | solution.py:100
  365.5 57.7 %all_to_all.15 = bf16[32,256,128]{2,1,0:T(8,128)(2,1)S(1)} all-to-all(bf16[32,256,128]{2,1,0:T(8,128)(2,1)} %fusion.2), channel_id=1, replica_groups=mesh['dp'=8,'mp'=32] {'mp'}, dimensions={0} | all-to-all | bytes 4194304 | tf_op jit(solution)/shard_map/all_to_all | solution.py:102
  423.3 1.3 copy.42
  (6 shorter events, 0.0 us)
Async XLA Ops:
  8.0 217.2 %copy-start = (bf16[4096,256]{1,0:T(8,128)(2,1)S(1)}, bf16[4096,256]{1,0:T(8,128)(2,1)}, u32[]{:S(2)}) copy-start(bf16[4096,256]{1,0:T(8,128)(2,1)} %param.17) | copy-start | bytes 6291460
  8.0 7.6 %copy-start.1 = (bf16[1,2048,128]{2,1,0:T(8,128)(2,1)S(1)}, bf16[1,2048,128]{2,1,0:T(8,128)(2,1)}, u32[]{:S(2)}) copy-start(bf16[1,2048,128]{2,1,0:T(8,128)(2,1)} %param.11) | copy-start | bytes 1572868
  118.8 93.0 %all-to-all-start = ((bf16[32,256,128]{2,1,0:T(8,128)(2,1)}), bf16[32,256,128]{2,1,0:T(8,128)(2,1)}, u32[]{:S(2)}, u32[]{:S(2)}) async-start(bf16[32,256,128]{2,1,0:T(8,128)(2,1)} %bitcast.116), calls=%async_computation | async-start | bytes 4194304 | tf_op jit(solution)/shard_map/all_to_all | solution.py:78
  130.5 81.3 %all-gather.2.cloned.1.call-start = ((), (), s32[]{:S(2)}) async-start(), calls=%async_computation.4 | async-start | bytes 1081344 | tf_op jit(solution)/shard_map/all_gather | solution.py:59
  217.3 6.5 %copy-start.2 = (bf16[256,1024]{1,0:T(8,128)(2,1)S(1)}, bf16[256,1024]{1,0:T(8,128)(2,1)}, u32[]{:S(2)}) copy-start(bf16[256,1024]{1,0:T(8,128)(2,1)} %param.16) | copy-start | bytes 1572868
  217.3 7.4 %copy-start.8 = (s32[1,8]{1,0:T(1,128)S(1)}, s32[1,8]{1,0:T(1,128)}, u32[]{:S(2)}) copy-start(s32[1,8]{1,0:T(1,128)} %param.13) | copy-start | bytes 100
  217.3 7.6 %copy-start.4 = (s32[256]{0:T(256)S(1)}, s32[256]{0:T(256)}, u32[]{:S(2)}) copy-start(s32[256]{0:T(256)} %param.14) | copy-start | bytes 3076
  217.3 99.4 %all-to-all-start.1 = ((bf16[8,4096,128]{2,1,0:T(8,128)(2,1)}), bf16[8,4096,128]{2,1,0:T(8,128)(2,1)}, u32[]{:S(2)}, u32[]{:S(2)}) async-start(bf16[8,4096,128]{2,1,0:T(8,128)(2,1)} %stack.2), calls=%async_computation.1 | async-start | bytes 16777216 | tf_op jit(solution)/shard_map/all_to_all | solution.py:61
  222.8 124.2 %reduce-scatter.2.cloned.1.call-start = ((), (), s32[]{:S(2)}) async-start(), calls=%async_computation.5 | async-start | bytes 147456 | tf_op jit(solution)/shard_map/reduce_scatter | solution.py:72
  327.0 13.3 %copy-start.3 = (f32[4096]{0:T(1024)S(1)}, f32[4096]{0:T(1024)}, u32[]{:S(2)}) copy-start(f32[4096]{0:T(1024)} %param.19) | copy-start | bytes 49156
  327.0 13.3 %copy-start.7 = (f32[1024]{0:T(1024)S(1)}, f32[1024]{0:T(1024)}, u32[]{:S(2)}) copy-start(f32[1024]{0:T(1024)} %param.21) | copy-start | bytes 12292
  347.1 1.6 copy-start.6
  348.3 7.5 %copy-start.5 = (f32[256]{0:T(256)}, f32[256]{0:T(256)S(1)}, u32[]{:S(2)}) copy-start(f32[256]{0:T(256)S(1)} %broadcast_multiply_fusion) | copy-start | bytes 3076
Sparse Core Ops, SparseCore 0:
  133.9 77.8 all-gather.1
Sparse Core Ops, SparseCore 1:
  226.4 29.6 reduce-scatter.1
